TPU v7x, 512 devices: a whole 4x4x16 slice. The times are simulated.
512 devices in a mesh: grp: 8 (over z_lo, core), spec: 64 (over z_hi, x, y).
Axes of the slice: x: 4, y: 4, z: 16 (z_hi: 4, z_lo: 4; z = z_hi * 4 + z_lo), core: 2. Of those that a mesh axis runs over, the one named last changes fastest.
Arguments:
- queries: bfloat16 [262144, 1024], P(('grp', 'spec')), may hold values from -6 to 6
- out_grad: bfloat16 [262144, 1024], P(('grp', 'spec')), may hold values from -48 to 48
- spec_keys: bfloat16 [512, 192, 1024], P(('grp', 'spec')), may hold values from -6 to 6
- spec_values: bfloat16 [512, 192, 1024], P(('grp', 'spec')), may hold values from -6 to 6
- owner_of: int32 [32768, 1], P(('grp', 'spec')), may hold values from 0 to 63; in each aligned block of 64 rows (0 to 63, 64 to 127, ...) at most 2 rows name the same one
- query_gain: float32 [1024], replicated, may hold values from 0.5 to 1.5
Outputs:
- query_grad: bfloat16 [262144, 1024], P(('grp', 'spec'))
- key_grad: bfloat16 [512, 192, 1024], P(('grp', 'spec'))
- value_grad: bfloat16 [512, 192, 1024], P(('grp', 'spec'))
- gain_grad: float32 [1024], replicated
Inputs may be any that keep to these rules, and one draw needn't show every extreme that they name: `owner_of`: among the candidates of one device, at most 2 name the same spec.
All inputs are finite; a program needn't handle non-finite values.
Results may differ from a plain program's by a relative error of at most 0.012.
The roundings to bfloat16 on the way count: a program that leaves them out, or rounds other values in their place, can miss the bound.
Values may be sent and summed in bfloat16 or wider, within the bound.
No kernel may reach another device: no remote copies, remote signals or barrier semaphores. Data moves between devices by JAX's collectives and lax.ppermute only.
A program may use at most 64 MiB of HBM per device.

v0:
```python
import math
import jax
import jax.numpy as jnp
from jax import lax
from jax.sharding import PartitionSpec as P

HEADS = 8
HEAD_DIM = 128
CAP = 2
PIECES = 2


def attend_backward(recv_rows, recv_grads, keys_here, values_here, query_gain):
    total_rows, _, head_dim = recv_rows.shape
    width = HEADS * head_dim
    key_count = keys_here.shape[0]
    inv_root = 1.0 / math.sqrt(HEAD_DIM)
    f32 = jnp.float32
    gain_hm = query_gain.reshape(HEADS, 1, head_dim)
    raw_hm = recv_rows.transpose(1, 0, 2)
    g_hm = recv_grads.transpose(1, 0, 2)
    k_hm = keys_here.reshape(key_count, HEADS, head_dim).transpose(1, 0, 2)
    v_hm = values_here.reshape(key_count, HEADS, head_dim).transpose(1, 0, 2)
    gained_hm = (raw_hm.astype(f32) * gain_hm).astype(jnp.bfloat16)
    scores = jnp.einsum("hrd,hkd->hrk", gained_hm, k_hm, preferred_element_type=f32) * inv_root
    top = jnp.max(scores, axis=2, keepdims=True)
    expo = jnp.exp(scores - top)
    probs = expo / jnp.sum(expo, axis=2, keepdims=True)
    probs_b = probs.astype(jnp.bfloat16)
    attended = jnp.einsum("hrk,hkd->hrd", probs_b, v_hm, preferred_element_type=f32)
    delta = jnp.sum(g_hm.astype(f32) * attended, axis=2, keepdims=True)
    dprobs = jnp.einsum("hrd,hkd->hrk", g_hm, v_hm, preferred_element_type=f32)
    dscores = (probs * (dprobs - delta)).astype(jnp.bfloat16)
    q_grad = jnp.einsum("hrk,hkd->hrd", dscores, k_hm, preferred_element_type=f32) * inv_root
    k_grad = jnp.einsum("hrk,hrd->hkd", dscores, gained_hm, preferred_element_type=f32) * inv_root
    v_grad = jnp.einsum("hrk,hrd->hkd", probs_b, g_hm, preferred_element_type=f32)
    gain_part = jnp.sum(raw_hm.astype(f32) * q_grad, axis=1).reshape(width)
    going_back = (q_grad * gain_hm).astype(jnp.bfloat16).transpose(1, 0, 2)
    key_grad = k_grad.astype(jnp.bfloat16).transpose(1, 0, 2).reshape(key_count, width)
    value_grad = v_grad.astype(jnp.bfloat16).transpose(1, 0, 2).reshape(key_count, width)
    return (going_back, gain_part, key_grad, value_grad)


def split_pieces(value, count):
    pieces = []
    rest = value
    for _ in range(count - 1):
        head = lax.reduce_precision(rest, exponent_bits=8, mantissa_bits=7)
        pieces.append(head)
        rest = rest - head
    pieces.append(rest)
    return jnp.stack(pieces).astype(jnp.bfloat16)


def shards(queries, out_grad, spec_keys, spec_values, owner_of, query_gain):
    peers = lax.axis_size("spec")
    cand_count = owner_of.shape[0]
    width = queries.shape[1]
    qtok_here = queries.shape[0] // cand_count
    slot_count = peers * CAP
    target = owner_of[:, 0]
    onehot = (target[:, None] == jnp.arange(peers, dtype=jnp.int32)[None, :]).astype(jnp.int32)
    earlier = jnp.cumsum(onehot, axis=0) - onehot
    position = jnp.sum(earlier * onehot, axis=1)
    slot_index = target * CAP + position
    matches = jnp.arange(slot_count, dtype=jnp.int32)[:, None] == slot_index[None, :]
    source = jnp.argmax(matches, axis=1).astype(jnp.int32)
    used = jnp.any(matches, axis=1)
    head_dim = width // HEADS
    both = jnp.concatenate(
        [
            queries.reshape(cand_count, qtok_here, HEADS, head_dim),
            out_grad.reshape(cand_count, qtok_here, HEADS, head_dim),
        ],
        axis=1,
    )
    both = jnp.pad(both, ((0, 1), (0, 0), (0, 0), (0, 0)))
    source = jnp.where(used, source, cand_count)
    send_both = jnp.take(both, source, axis=0, mode="clip")
    send_both = send_both.reshape(peers, CAP * 2 * qtok_here, HEADS, head_dim)
    recv_both = lax.all_to_all(send_both, "spec", split_axis=0, concat_axis=0, tiled=True)
    recv_both = recv_both.reshape(slot_count, 2, qtok_here, HEADS, head_dim)
    recv_rows = recv_both[:, 0].reshape(slot_count * qtok_here, HEADS, head_dim)
    recv_cotan = recv_both[:, 1].reshape(slot_count * qtok_here, HEADS, head_dim)
    going_back, partial_value, key_grad, value_grad = attend_backward(
        recv_rows, recv_cotan, spec_keys[0], spec_values[0], query_gain
    )
    going_back = going_back.reshape(peers, CAP * qtok_here, HEADS, width // HEADS)
    gain_rows = jnp.broadcast_to(
        split_pieces(partial_value, PIECES).reshape(1, PIECES, HEADS, width // HEADS),
        (peers, PIECES, HEADS, width // HEADS),
    )
    going_back = jnp.concatenate([going_back, gain_rows], axis=1)
    came_back = lax.all_to_all(going_back, "spec", split_axis=0, concat_axis=0, tiled=True)
    spec_sum = jnp.sum(came_back[:, CAP * qtok_here :].astype(jnp.float32), axis=(0, 1)).reshape(
        width
    )
    gain_grad = lax.psum(spec_sum, "grp")
    came_back = came_back[:, : CAP * qtok_here]
    home_grads = jnp.take(
        came_back.reshape(slot_count, qtok_here, HEADS, width // HEADS),
        slot_index,
        axis=0,
        mode="clip",
    )
    query_grad = home_grads.reshape(cand_count * qtok_here, width)
    return (query_grad, key_grad[None], value_grad[None], gain_grad)


def solution(mesh):
    return jax.shard_map(
        shards,
        mesh=mesh,
        in_specs=(
            P(("grp", "spec"), None),
            P(("grp", "spec"), None),
            P(("grp", "spec"), None, None),
            P(("grp", "spec"), None, None),
            P(("grp", "spec"), None),
            P(),
        ),
        out_specs=(
            P(("grp", "spec"), None),
            P(("grp", "spec"), None, None),
            P(("grp", "spec"), None, None),
            P(),
        ),
        check_vma=False,
    )
```

profile of v0, /device:TPU:1, one launch (start us, length us, event | category | flops | bytes accessed | tf_op | source)
XLA Modules:
  0.0 385.1 jit_solution(2665026931376670259)
XLA Ops:
  0.6 0.7 fusion.36
  1.4 0.1 reduce_window_sum.11
  1.5 0.8 select_reduce_fusion
  2.3 0.7 multiply_add_fusion
  3.0 0.6 iota_reduce_fusion
  3.7 2.2 copy_bitcast_fusion.1
  5.9 0.2 fusion.10
  6.1 3.1 gather_fusion
  9.1 22.3 %all-to-all-start = ((bf16[64,32,8,128]{3,2,1,0:T(8,128)(2,1)}), bf16[64,32,8,128]{3,2,1,0:T(8,128)(2,1)}, u32[]{:S(2)}, u32[]{:S(2)}) async-start(bf16[64,32,8,128]{3,2,1,0:T(8,128)(2,1)} %bitcast.82), calls=%async_computation | async-start | bytes 8388608 | tf_op jit(solution)/shard_map/all_to_all | solution.py:81
  31.6 184.3 %all-to-all-done = bf16[64,32,8,128]{3,2,1,0:T(8,128)(2,1)} async-done(((bf16[64,32,8,128]{3,2,1,0:T(8,128)(2,1)}), bf16[64,32,8,128]{3,2,1,0:T(8,128)(2,1)}, u32[]{:S(2)}, u32[]{:S(2)}) %all-to-all-start) | async-done | bytes 4194336 | tf_op jit(solution)/shard_map/all_to_all | solution.py:81
  215.9 3.1 fusion.41
  219.0 1.4 fusion.25
  220.4 5.1 %fusion.42 = (f32[8,1024]{1,0:T(8,128)S(1)}, f32[8,1024,192]{1,2,0:T(8,128)S(1)}) fusion(f32[8,1024,192]{1,2,0:T(8,128)S(1)} %fusion.25), kind=kOutput, calls=%fused_computation.65 | output fusion | flops 6291647 | bytes 12615680 | tf_op jit(solution)/shard_map/sub | solution.py:27
  225.5 1.0 fusion.9
  226.5 2.3 multiply_reduce_fusion.1
  228.9 2.3 multiply_convert_fusion
  231.2 2.0 multiply_convert_fusion.1
  233.2 2.4 copy.40
  235.8 1.6 pad_maximum_fusion
  237.4 15.2 %all-to-all-start.1 = ((bf16[64,18,8,128]{3,2,1,0:T(8,128)(2,1)}), bf16[64,18,8,128]{3,2,1,0:T(8,128)(2,1)}, u32[]{:S(2)}, u32[]{:S(2)}) async-start(bf16[64,18,8,128]{3,2,1,0:T(8,128)(2,1)} %pad_maximum_fusion), calls=%async_computation.1 | async-start | bytes 4718592 | tf_op jit(solution)/shard_map/all_to_all | solution.py:94
  252.6 3.6 fusion.20
  256.2 0.3 copy.41
  256.5 0.9 broadcast_in_dim_reshape.6
  257.4 3.7 fusion.21
  261.1 0.3 copy.42
  261.4 0.9 broadcast_in_dim_reshape.7
  262.3 96.9 %all-to-all-done.1 = bf16[64,18,8,128]{3,2,1,0:T(8,128)(2,1)} async-done(((bf16[64,18,8,128]{3,2,1,0:T(8,128)(2,1)}), bf16[64,18,8,128]{3,2,1,0:T(8,128)(2,1)}, u32[]{:S(2)}, u32[]{:S(2)}) %all-to-all-start.1) | async-done | bytes 2359328 | tf_op jit(solution)/shard_map/all_to_all | solution.py:94
  359.2 1.7 slice.22
  360.9 0.7 gather_fusion.1
  361.7 1.2 copy.87
  362.9 1.1 convert_reduce_fusion
  364.0 21.0 %psum.7 = f32[1024]{0:T(1024)} all-reduce(f32[1024]{0:T(1024)S(1)} %bitcast.96), channel_id=1, replica_groups=mesh['grp'=8,'spec'=64] {'grp'}, use_global_device_ids=true, to_apply=%region_9.10 | all-reduce | flops 1024 | bytes 8192 | tf_op jit(solution)/shard_map/psum | solution.py:98
  (27 shorter events, 0.3 us)
Async XLA Ops:
  9.1 22.3 %copy-start.3 = (bf16[1,192,1024]{2,1,0:T(8,128)(2,1)S(1)}, bf16[1,192,1024]{2,1,0:T(8,128)(2,1)}, u32[]{:S(2)}) copy-start(bf16[1,192,1024]{2,1,0:T(8,128)(2,1)} %param.8) | copy-start | bytes 1179652
  9.1 22.4 %copy-start.4 = (bf16[1,192,1024]{2,1,0:T(8,128)(2,1)S(1)}, bf16[1,192,1024]{2,1,0:T(8,128)(2,1)}, u32[]{:S(2)}) copy-start(bf16[1,192,1024]{2,1,0:T(8,128)(2,1)} %param.9) | copy-start | bytes 1179652
  9.1 22.5 %copy-start.6 = (f32[1024]{0:T(1024)S(1)}, f32[1024]{0:T(1024)}, u32[]{:S(2)}) copy-start(f32[1024]{0:T(1024)} %param.11) | copy-start | bytes 12292
  9.1 206.8 %all-to-all-start = ((bf16[64,32,8,128]{3,2,1,0:T(8,128)(2,1)}), bf16[64,32,8,128]{3,2,1,0:T(8,128)(2,1)}, u32[]{:S(2)}, u32[]{:S(2)}) async-start(bf16[64,32,8,128]{3,2,1,0:T(8,128)(2,1)} %bitcast.82), calls=%async_computation | async-start | bytes 8388608 | tf_op jit(solution)/shard_map/all_to_all | solution.py:81
  31.6 194.9 %copy-start.5 = (bf16[24,8,8,128]{3,2,1,0:T(8,128)(2,1)}, bf16[24,8,8,128]{3,2,1,0:T(8,128)(2,1)S(1)}, u32[]{:S(2)}) copy-start(bf16[24,8,8,128]{3,2,1,0:T(8,128)(2,1)S(1)} %copy.47) | copy-start | bytes 1179652
  219.0 9.9 %copy-start.2 = (bf16[128,1,8,8,128]{4,3,2,1,0:T(8,128)(2,1)}, bf16[128,1,8,8,128]{4,3,2,1,0:T(8,128)(2,1)S(1)}, u32[]{:S(2)}) copy-start(bf16[128,1,8,8,128]{4,3,2,1,0:T(8,128)(2,1)S(1)} %get-tuple-element.8) | copy-start | bytes 6291460
  219.0 12.2 %copy-start = (f32[128,1,8,8,128]{4,3,2,1,0:T(8,128)}, f32[128,1,8,8,128]{4,3,2,1,0:T(8,128)S(1)}, u32[]{:S(2)}) copy-start(f32[128,1,8,8,128]{4,3,2,1,0:T(8,128)S(1)} %get-tuple-element.9) | copy-start | bytes 12582916
  226.5 4.7 %copy-start.1 = (bf16[8,1024,192]{1,2,0:T(8,128)(2,1)}, bf16[8,1024,192]{1,2,0:T(8,128)(2,1)S(1)}, u32[]{:S(2)}) copy-start(bf16[8,1024,192]{1,2,0:T(8,128)(2,1)S(1)} %fusion.9) | copy-start | bytes 9437188
  235.7 16.8 %copy-start.7 = (s32[64,1]{0,1:T(1,128)S(1)}, s32[64,1]{0,1:T(1,128)}, u32[]{:S(2)}) copy-start(s32[64,1]{0,1:T(1,128)} %param.10) | copy-start | bytes 772
  237.4 121.8 %all-to-all-start.1 = ((bf16[64,18,8,128]{3,2,1,0:T(8,128)(2,1)}), bf16[64,18,8,128]{3,2,1,0:T(8,128)(2,1)}, u32[]{:S(2)}, u32[]{:S(2)}) async-start(bf16[64,18,8,128]{3,2,1,0:T(8,128)(2,1)} %pad_maximum_fusion), calls=%async_computation.1 | async-start | bytes 4718592 | tf_op jit(solution)/shard_map/all_to_all | solution.py:94
where the time goes:
time: 386 us; the launch traced here: 385 us
  waiting for transfers between devices  281 us (73%)
  starting transfers between devices  37.5 us (10%)
  blocking collectives  21 us (5%)
  matrix products  15.4 us (4%)
  other arithmetic  15.1 us (4%)
  local copies, waits for them, and re-layouts  13.9 us (4%)
    all_to_all x1, waiting for transfers between devices, shards(): lax.all_to_all(send_both, 'spec', split_axis=0, concat_axis=0, tiled=True)  184 us
    all_to_all x1, waiting for transfers between devices, shards(): lax.all_to_all(going_back, 'spec', split_axis=0, concat_axis=0, tiled=True)  96.9 us
    all_to_all x1, starting transfers between devices, shards(): lax.all_to_all(send_both, 'spec', split_axis=0, concat_axis=0, tiled=True)  22.3 us
    psum x1, blocking collectives, shards(): gain_grad = lax.psum(spec_sum, 'grp')  21 us
    all_to_all x1, starting transfers between devices, shards(): lax.all_to_all(going_back, 'spec', split_axis=0, concat_axis=0, tiled=True)  15.2 us
  transfers between devices with their start and end apart: 2, of which 2 were waited for; matrix products, arithmetic and copies ran while one was open for 3% of the time, Pallas kernels for 0%

commit v1 on v0

--- a/solution.py
+++ b/solution.py
@@ -3,6 +3,7 @@
 import jax.numpy as jnp
 from jax import lax
 from jax.sharding import PartitionSpec as P
+from jax.lax import all_gather
 
 HEADS = 8
 HEAD_DIM = 128
@@ -53,6 +54,11 @@
 
 
 def shards(queries, out_grad, spec_keys, spec_values, owner_of, query_gain):
+
+    def save_the_sheet(x_in, axis_key="grp"):
+        k_now = all_gather(x_in, axis_key)
+        return jnp.sum(k_now, 0)
+
     peers = lax.axis_size("spec")
     cand_count = owner_of.shape[0]
     width = queries.shape[1]
@@ -95,7 +101,7 @@
     spec_sum = jnp.sum(came_back[:, CAP * qtok_here :].astype(jnp.float32), axis=(0, 1)).reshape(
         width
     )
-    gain_grad = lax.psum(spec_sum, "grp")
+    gain_grad = save_the_sheet(spec_sum)
     came_back = came_back[:, : CAP * qtok_here]
     home_grads = jnp.take(
         came_back.reshape(slot_count, qtok_here, HEADS, width // HEADS),

time: 386 us -> 387 us (level)
    all_gather x0 -> x1, blocking collectives: none -> 21.8 us  [save_the_sheet(): k_now = all_gather(x_in, axis_key)]
    psum x1 -> x0, blocking collectives: 21 us -> none  [shards(): gain_grad = lax.psum(spec_sum, 'grp')]
where the time goes in v1:
time: 387 us; the launch traced here: 386 us
  waiting for transfers between devices  281 us (73%)
  starting transfers between devices  37.5 us (10%)
  blocking collectives  21.8 us (6%)
  other arithmetic  15.7 us (4%)
  matrix products  15.4 us (4%)
  local copies, waits for them, and re-layouts  13.9 us (4%)
    all_to_all x1, waiting for transfers between devices, shards(): lax.all_to_all(send_both, 'spec', split_axis=0, concat_axis=0, tiled=True)  184 us
    all_to_all x1, waiting for transfers between devices, shards(): lax.all_to_all(going_back, 'spec', split_axis=0, concat_axis=0, tiled=True)  96.9 us
    all_to_all x1, starting transfers between devices, shards(): lax.all_to_all(send_both, 'spec', split_axis=0, concat_axis=0, tiled=True)  22.3 us
    all_gather x1, blocking collectives, save_the_sheet(): k_now = all_gather(x_in, axis_key)  21.8 us
    all_to_all x1, starting transfers between devices, shards(): lax.all_to_all(going_back, 'spec', split_axis=0, concat_axis=0, tiled=True)  15.2 us
  transfers between devices with their start and end apart: 2, of which 2 were waited for; matrix products, arithmetic and copies ran while one was open for 3% of the time, Pallas kernels for 0%

profile of v1, /device:TPU:1, one launch (start us, length us, event | category | flops | bytes accessed | tf_op | source)
XLA Modules:
  0.0 386.4 jit_solution(14655806935987668711)
XLA Ops:
  0.6 0.7 fusion.36
  1.5 0.8 select_reduce_fusion
  2.3 0.7 multiply_add_fusion
  3.0 0.6 iota_reduce_fusion
  3.7 2.2 copy_bitcast_fusion.1
  5.9 0.2 fusion.10
  6.1 3.1 gather_fusion
  9.1 22.3 %all-to-all-start = ((bf16[64,32,8,128]{3,2,1,0:T(8,128)(2,1)}), bf16[64,32,8,128]{3,2,1,0:T(8,128)(2,1)}, u32[]{:S(2)}, u32[]{:S(2)}) async-start(bf16[64,32,8,128]{3,2,1,0:T(8,128)(2,1)} %bitcast.82), calls=%async_computation | async-start | bytes 8388608 | tf_op jit(solution)/shard_map/all_to_all | solution.py:87
  31.6 184.3 %all-to-all-done = bf16[64,32,8,128]{3,2,1,0:T(8,128)(2,1)} async-done(((bf16[64,32,8,128]{3,2,1,0:T(8,128)(2,1)}), bf16[64,32,8,128]{3,2,1,0:T(8,128)(2,1)}, u32[]{:S(2)}, u32[]{:S(2)}) %all-to-all-start) | async-done | bytes 4194336 | tf_op jit(solution)/shard_map/all_to_all | solution.py:87
  215.9 3.1 fusion.41
  219.0 1.4 fusion.25
  220.4 5.1 %fusion.42 = (f32[8,1024]{1,0:T(8,128)S(1)}, f32[8,1024,192]{1,2,0:T(8,128)S(1)}) fusion(f32[8,1024,192]{1,2,0:T(8,128)S(1)} %fusion.25), kind=kOutput, calls=%fused_computation.65 | output fusion | flops 6291647 | bytes 12615680 | tf_op jit(solution)/shard_map/sub | solution.py:28
  225.5 1.0 fusion.9
  226.5 2.3 multiply_reduce_fusion.1
  228.9 2.3 multiply_convert_fusion
  231.2 2.0 multiply_convert_fusion.1
  233.2 2.4 copy.40
  235.8 1.6 pad_maximum_fusion
  237.4 15.2 %all-to-all-start.1 = ((bf16[64,18,8,128]{3,2,1,0:T(8,128)(2,1)}), bf16[64,18,8,128]{3,2,1,0:T(8,128)(2,1)}, u32[]{:S(2)}, u32[]{:S(2)}) async-start(bf16[64,18,8,128]{3,2,1,0:T(8,128)(2,1)} %pad_maximum_fusion), calls=%async_computation.1 | async-start | bytes 4718592 | tf_op jit(solution)/shard_map/all_to_all | solution.py:100
  252.6 3.6 fusion.20
  256.2 0.3 copy.41
  256.5 0.9 broadcast_in_dim_reshape.6
  257.4 3.7 fusion.21
  261.1 0.3 copy.42
  261.4 0.9 broadcast_in_dim_reshape.7
  262.3 96.9 %all-to-all-done.1 = bf16[64,18,8,128]{3,2,1,0:T(8,128)(2,1)} async-done(((bf16[64,18,8,128]{3,2,1,0:T(8,128)(2,1)}), bf16[64,18,8,128]{3,2,1,0:T(8,128)(2,1)}, u32[]{:S(2)}, u32[]{:S(2)}) %all-to-all-start.1) | async-done | bytes 2359328 | tf_op jit(solution)/shard_map/all_to_all | solution.py:100
  359.2 1.7 slice.22
  360.9 0.7 gather_fusion.1
  361.7 1.2 copy.87
  362.9 1.1 convert_reduce_fusion
  364.0 21.8 %all-gather = f32[8,1,1024]{2,1,0:T(1,128)S(1)} all-gather(f32[1,1,1024]{2,1,0:T(1,128)S(1)} %bitcast.96), channel_id=1, replica_groups=mesh['grp'=8,'spec'=64] {'grp'}, dimensions={0}, use_global_device_ids=true | all-gather | bytes 36864 | tf_op jit(solution)/shard_map/all_gather | solution.py:59
  385.8 0.6 reduce_sum.65
  (28 shorter events, 0.4 us)
Async XLA Ops:
  9.1 22.3 %copy-start.3 = (bf16[1,192,1024]{2,1,0:T(8,128)(2,1)S(1)}, bf16[1,192,1024]{2,1,0:T(8,128)(2,1)}, u32[]{:S(2)}) copy-start(bf16[1,192,1024]{2,1,0:T(8,128)(2,1)} %param.8) | copy-start | bytes 1179652
  9.1 22.4 %copy-start.4 = (bf16[1,192,1024]{2,1,0:T(8,128)(2,1)S(1)}, bf16[1,192,1024]{2,1,0:T(8,128)(2,1)}, u32[]{:S(2)}) copy-start(bf16[1,192,1024]{2,1,0:T(8,128)(2,1)} %param.9) | copy-start | bytes 1179652
  9.1 22.5 %copy-start.6 = (f32[1024]{0:T(1024)S(1)}, f32[1024]{0:T(1024)}, u32[]{:S(2)}) copy-start(f32[1024]{0:T(1024)} %param.11) | copy-start | bytes 12292
  9.1 206.8 %all-to-all-start = ((bf16[64,32,8,128]{3,2,1,0:T(8,128)(2,1)}), bf16[64,32,8,128]{3,2,1,0:T(8,128)(2,1)}, u32[]{:S(2)}, u32[]{:S(2)}) async-start(bf16[64,32,8,128]{3,2,1,0:T(8,128)(2,1)} %bitcast.82), calls=%async_computation | async-start | bytes 8388608 | tf_op jit(solution)/shard_map/all_to_all | solution.py:87
  31.6 194.9 %copy-start.5 = (bf16[24,8,8,128]{3,2,1,0:T(8,128)(2,1)}, bf16[24,8,8,128]{3,2,1,0:T(8,128)(2,1)S(1)}, u32[]{:S(2)}) copy-start(bf16[24,8,8,128]{3,2,1,0:T(8,128)(2,1)S(1)} %copy.47) | copy-start | bytes 1179652
  219.0 9.9 %copy-start.2 = (bf16[128,1,8,8,128]{4,3,2,1,0:T(8,128)(2,1)}, bf16[128,1,8,8,128]{4,3,2,1,0:T(8,128)(2,1)S(1)}, u32[]{:S(2)}) copy-start(bf16[128,1,8,8,128]{4,3,2,1,0:T(8,128)(2,1)S(1)} %get-tuple-element.8) | copy-start | bytes 6291460
  219.0 12.2 %copy-start = (f32[128,1,8,8,128]{4,3,2,1,0:T(8,128)}, f32[128,1,8,8,128]{4,3,2,1,0:T(8,128)S(1)}, u32[]{:S(2)}) copy-start(f32[128,1,8,8,128]{4,3,2,1,0:T(8,128)S(1)} %get-tuple-element.9) | copy-start | bytes 12582916
  226.5 4.7 %copy-start.1 = (bf16[8,1024,192]{1,2,0:T(8,128)(2,1)}, bf16[8,1024,192]{1,2,0:T(8,128)(2,1)S(1)}, u32[]{:S(2)}) copy-start(bf16[8,1024,192]{1,2,0:T(8,128)(2,1)S(1)} %fusion.9) | copy-start | bytes 9437188
  235.7 16.8 %copy-start.7 = (s32[64,1]{0,1:T(1,128)S(1)}, s32[64,1]{0,1:T(1,128)}, u32[]{:S(2)}) copy-start(s32[64,1]{0,1:T(1,128)} %param.10) | copy-start | bytes 772
  237.4 121.8 %all-to-all-start.1 = ((bf16[64,18,8,128]{3,2,1,0:T(8,128)(2,1)}), bf16[64,18,8,128]{3,2,1,0:T(8,128)(2,1)}, u32[]{:S(2)}, u32[]{:S(2)}) async-start(bf16[64,18,8,128]{3,2,1,0:T(8,128)(2,1)} %pad_maximum_fusion), calls=%async_computation.1 | async-start | bytes 4718592 | tf_op jit(solution)/shard_map/all_to_all | solution.py:100
